TPU v7x, 32 devices: a whole 2x2x4 slice. The times are simulated.
32 devices in a mesh: seq: 8 (over y, x, core), chan: 4 (over z).
Axes of the slice: x: 2, y: 2, z: 4, core: 2. Of those that a mesh axis runs over, the one named last changes fastest.
Arguments:
- query_proj: bfloat16 [1024, 8192], P('seq', 'chan'), may hold values from -8 to 8
- key_proj: bfloat16 [1024, 8192], P('seq', 'chan'), may hold values from -8 to 8
- value_proj: bfloat16 [1024, 8192], P('seq', 'chan'), may hold values from -6 to 6
- residual: bfloat16 [1024, 8192], P('seq', 'chan'), may hold values from -6 to 6
- out_weight: bfloat16 [8192, 8192], P('chan', 'seq'), may hold values from -0.0625 to 0.0625
Outputs:
- attn_out: bfloat16 [1024, 8192], P('seq', 'chan')
All inputs are finite; a program needn't handle non-finite values.
Results may differ from a plain program's by a relative error of at most 0.008.
Values may be sent and summed in bfloat16 or wider, within the bound.
No kernel may reach another device: no remote copies, remote signals or barrier semaphores. Data moves between devices by JAX's collectives and lax.ppermute only.
A program may use at most 64 MiB of HBM per device.

v0:
```python
import math
import jax
import jax.numpy as jnp
from jax import lax
from jax.sharding import PartitionSpec as P

HEAD_DIM = 128


def attend(state, query_rows, first_pos, key_block, value_block, block_start, score_scale):
    row_max, row_total, accum = state
    scores = (
        jnp.einsum("qhd,khd->hqk", query_rows, key_block, preferred_element_type=jnp.float32)
        * score_scale
    )
    row_pos = first_pos + jnp.arange(query_rows.shape[0], dtype=jnp.int32)
    col_pos = block_start + jnp.arange(key_block.shape[0], dtype=jnp.int32)
    allowed = (col_pos[None, :] <= row_pos[:, None])[None]
    scores = jnp.where(allowed, scores, -1e30)
    new_max = jnp.maximum(row_max, jnp.max(scores, axis=-1))
    weights = jnp.where(allowed, jnp.exp(scores - new_max[..., None]), 0.0)
    factor = jnp.exp(row_max - new_max)
    row_total = row_total * factor + jnp.sum(weights, axis=-1)
    accum = accum * factor[..., None] + jnp.einsum(
        "hqk,khd->hqd",
        weights.astype(jnp.bfloat16),
        value_block,
        preferred_element_type=jnp.float32,
    )
    return (new_max, row_total, accum)


def guarded(state, query_rows, first_pos, key_block, value_block, block_start, score_scale):
    last_pos = first_pos + query_rows.shape[0] - 1

    def do_update(inner):
        return attend(
            inner, query_rows, first_pos, key_block, value_block, block_start, score_scale
        )

    def keep_state(inner):
        return inner

    return lax.cond(block_start <= last_pos, do_update, keep_state, state)


def per_device(query_proj, key_proj, value_proj, residual, out_weight):
    seg_rows = query_proj.shape[0]
    feat_width = query_proj.shape[1]
    heads_here = feat_width // HEAD_DIM
    seq_count = lax.axis_size("seq")
    chan_count = lax.axis_size("chan")
    segment = lax.axis_index("seq")
    score_scale = 1.0 / math.sqrt(HEAD_DIM)
    groups = [(query_proj, segment * seg_rows)]
    shaped = [
        (rows.reshape(rows.shape[0], heads_here, HEAD_DIM), first_pos) for rows, first_pos in groups
    ]
    starting = tuple(
        (
            (
                jnp.full((heads_here, rows.shape[0]), -1e30, jnp.float32),
                jnp.zeros((heads_here, rows.shape[0]), jnp.float32),
                jnp.zeros((heads_here, rows.shape[0], HEAD_DIM), jnp.float32),
            )
            for rows, first_pos in shaped
        )
    )
    piece_keys = lax.all_gather(key_proj, "seq", axis=0, tiled=True)
    piece_values = lax.all_gather(value_proj, "seq", axis=0, tiled=True)
    piece_rows = piece_keys.shape[0]

    def one_block(block_index, states):
        offset = block_index * seg_rows
        key_block = lax.dynamic_slice_in_dim(piece_keys, offset, seg_rows, 0).reshape(
            seg_rows, heads_here, HEAD_DIM
        )
        value_block = lax.dynamic_slice_in_dim(piece_values, offset, seg_rows, 0).reshape(
            seg_rows, heads_here, HEAD_DIM
        )
        updated = []
        for (query_rows, first_pos), state in zip(shaped, states):
            updated.append(
                guarded(state, query_rows, first_pos, key_block, value_block, offset, score_scale)
            )
        return tuple(updated)

    finals = lax.fori_loop(0, piece_rows // seg_rows, one_block, starting)
    pieces_out = []
    for row_max, row_total, accum in finals:
        ratio = accum / row_total[..., None]
        pieces_out.append(
            ratio.transpose(1, 0, 2).reshape(ratio.shape[1], feat_width).astype(jnp.bfloat16)
        )
    local_context = pieces_out[0]
    gathered = lax.all_gather(local_context, "seq", axis=0, tiled=True)
    sub_rows = seg_rows // chan_count
    grid = gathered.reshape(seq_count, chan_count, sub_rows, feat_width)
    block_tokens = seq_count * sub_rows
    rows = grid.transpose(1, 0, 2, 3).reshape(block_tokens * lax.axis_size("chan"), feat_width)
    partial_sums = lax.psum_scatter(
        jnp.dot(rows, out_weight, preferred_element_type=jnp.float32).astype(jnp.bfloat16),
        "chan",
        scatter_dimension=0,
        tiled=True,
    ).astype(jnp.float32)
    relaid = lax.all_to_all(
        lax.all_to_all(
            partial_sums.astype(jnp.bfloat16), "seq", split_axis=0, concat_axis=1, tiled=True
        ),
        "chan",
        split_axis=1,
        concat_axis=0,
        tiled=True,
    ).astype(partial_sums.dtype)
    return (residual.astype(jnp.float32) + relaid).astype(jnp.bfloat16)


def solution(mesh):
    placed = (
        P("seq", "chan"),
        P("seq", "chan"),
        P("seq", "chan"),
        P("seq", "chan"),
        P("chan", "seq"),
    )
    return jax.shard_map(
        per_device, mesh=mesh, in_specs=placed, out_specs=P("seq", "chan"), check_vma=False
    )
```

profile of v0, /device:TPU:0, one launch (start us, length us, event | category | flops | bytes accessed | tf_op | source)
XLA Modules:
  0.0 250.2 jit_solution(13693621716920695424)
XLA Ops:
  6.5 0.0 all-gather.4.cloned.1.call-start
  6.5 2.0 copy.32
  8.6 0.0 all-gather.4.cloned.1.call-update
  8.6 0.0 all-gather.6.cloned.1.call-start
  8.7 2.1 copy.34
  10.7 0.0 all-gather.6.cloned.1.call-update
  10.8 0.0 all-gather.8.cloned.1.call-start
  10.8 1.3 copy.33
  12.1 0.3 copy.35
  12.4 37.0 %all-gather.4.cloned.1.call-done = bf16[1024,2048]{0,1:T(8,128)(2,1)} async-done(((bf16[128,2048]{0,1:T(8,128)(2,1)}), bf16[1024,2048]{0,1:T(8,128)(2,1)}) %all-gather.4.cloned.1.call-update) | async-done | bytes 4194320 | tf_op jit(solution)/shard_map/all_gather | solution.py:69
  49.4 39.3 %all-gather.6.cloned.1.call-done = bf16[1024,2048]{0,1:T(8,128)(2,1)} async-done(((bf16[128,2048]{0,1:T(8,128)(2,1)}), bf16[1024,2048]{0,1:T(8,128)(2,1)}) %all-gather.6.cloned.1.call-update) | async-done | bytes 4194320 | tf_op jit(solution)/shard_map/all_gather | solution.py:70
  88.8 0.1 broadcast_in_dim.45
  88.9 3.3 %while.19 = (s32[]{:T(128)}, f32[16,128]{1,0:T(8,128)S(1)}, f32[16,128]{1,0:T(8,128)S(1)}, f32[16,128,128]{2,1,0:T(8,128)S(1)}, s32[]{:T(128)}, /*index=5*/s32[]...) while((s32[]{:T(128)}, f32[16,128]{1,0:T(8,128)S(1)}, ...), condition=%wide.region_5.6_spmd, body=%wide.region_0.5_spmd.sunk | while | flops 137122048 | bytes 9111853 | solution.py:88
  88.9 3.0 %conditional.2 = ((f32[16,128]{1,0:T(8,128)S(1)}, f32[16,128]{1,0:T(8,128)S(1)}, f32[16,128,128]{2,1,0:T(8,128)S(1)})) conditional(s32[]{:T(128)} %convert_element_type.63, (f32[16,128]{1,0:T(8,128)S(1)}, f32[16,128]{1,0:T(8,128)S(1)}, f32[16,128,128]{2,1,0:T(8,128)S(1)}) %tuple.61, (s32[]{:T(128)}, s32[]{:T(128)}, bf16[1024,2048]{0,1:T(8,128)(2,1)}, ...), branch_computations={%region_1.0_spmd, %region_2.4_spmd} | conditional | flops 137122048 | bytes 9111630 | solution.py:44
  88.9 1.3 constant_dynamic-slice_fusion
  90.2 0.1 broadcast_compare_fusion
  90.3 0.5 fusion.10
  90.8 0.2 fusion.3
  91.1 0.8 convolution_add_fusion
  92.2 0.3 copy.36
  92.5 0.9 divide_convert_fusion
  93.5 0.0 all-gather.8.cloned.1.call-update
  93.5 0.0 reduce-scatter.2.cloned.1.call-start
  93.5 58.4 %all-gather.8.cloned.1.call-done = bf16[1024,2048]{0,1:T(8,128)(2,1)} async-done(((bf16[128,2048]{0,1:T(8,128)(2,1)}), bf16[1024,2048]{0,1:T(8,128)(2,1)}) %all-gather.8.cloned.1.call-update) | async-done | bytes 4194320 | tf_op jit(solution)/shard_map/all_gather | solution.py:96
  151.9 6.5 %copy.37 = bf16[1024,2048]{1,0:T(8,128)(2,1)} copy(bf16[1024,2048]{0,1:T(8,128)(2,1)} %all-gather.8.cloned.1.call-done) | data formatting | bytes 8388608 | tf_op jit(solution)/shard_map/all_gather | solution.py:96
  158.4 0.0 copy-start.1
  158.4 2.7 %copy.38 = bf16[4,8,32,2048]{3,2,1,0:T(8,128)(2,1)S(1)} copy(bf16[4,8,32,2048]{3,2,0,1:T(8,128)(2,1)} %bitcast.29) | data formatting | bytes 8388608 | tf_op jit(solution)/shard_map/transpose | solution.py:100
  161.1 0.8 copy-done.1
  161.9 5.7 %convolution_convert_fusion = bf16[1024,1024]{1,0:T(8,128)(2,1)} fusion(bf16[1024,2048]{1,0:T(8,128)(2,1)S(1)} %bitcast.30, bf16[2048,1024]{1,0:T(8,128)(2,1)S(1)} %copy-done.1), kind=kOutput, calls=%fused_computation.18 | convolution fusion | flops 4296015872 | bytes 10485760 | tf_op jit(solution)/shard_map/dot_general | solution.py:102
  167.6 0.0 copy-start
  167.6 0.0 reduce-scatter.2.cloned.1.call-update
  167.7 44.0 %reduce-scatter.2.cloned.1.call-done = bf16[256,1024]{1,0:T(8,128)(2,1)} async-done(((bf16[1024,1024]{1,0:T(8,128)(2,1)}), bf16[256,1024]{1,0:T(8,128)(2,1)}) %reduce-scatter.2.cloned.1.call-update) | async-done | bytes 524304 | tf_op jit(solution)/shard_map/reduce_scatter | solution.py:101
  211.7 13.4 %all_to_all.29 = bf16[8,32,1024]{2,1,0:T(8,128)(2,1)S(1)} all-to-all(bf16[8,32,1024]{2,1,0:T(8,128)(2,1)} %bitcast.34), channel_id=1, replica_groups=mesh['seq'=8,'chan'=4] {'seq'}, dimensions={0} | all-to-all | bytes 1048576 | tf_op jit(solution)/shard_map/all_to_all | solution.py:108
  225.1 0.3 copy.39
  225.3 0.4 all_to_all.25
  225.7 0.3 copy.40
  226.0 16.7 %all_to_all.30 = bf16[32,4,2048]{2,0,1:T(8,128)(2,1)S(1)} all-to-all(bf16[32,4,2048]{2,0,1:T(8,128)(2,1)S(1)} %copy.40), channel_id=1, replica_groups=mesh['seq'=8,'chan'=4] {'chan'}, dimensions={1} | all-to-all | bytes 1048576 | tf_op jit(solution)/shard_map/all_to_all | solution.py:107
  242.7 0.0 copy-done
  242.7 0.9 fusion.9
  (13 shorter events, 0.1 us)
Async XLA Ops:
  6.5 42.9 %all-gather.4.cloned.1.call-start = ((), (), s32[]{:S(2)}) async-start(), calls=%async_computation.3 | async-start | bytes 4718592 | tf_op jit(solution)/shard_map/all_gather | solution.py:69
  8.6 80.1 %all-gather.6.cloned.1.call-start = ((), (), s32[]{:S(2)}) async-start(), calls=%async_computation.4 | async-start | bytes 4718592 | tf_op jit(solution)/shard_map/all_gather | solution.py:70
  10.8 141.2 %all-gather.8.cloned.1.call-start = ((), (), s32[]{:S(2)}) async-start(), calls=%async_computation.5 | async-start | bytes 4718592 | tf_op jit(solution)/shard_map/all_gather | solution.py:96
  93.5 118.2 %reduce-scatter.2.cloned.1.call-start = ((), (), s32[]{:S(2)}) async-start(), calls=%async_computation.6 | async-start | bytes 2621440 | tf_op jit(solution)/shard_map/reduce_scatter | solution.py:101
  158.4 3.4 %copy-start.1 = (bf16[2048,1024]{1,0:T(8,128)(2,1)S(1)}, bf16[2048,1024]{1,0:T(8,128)(2,1)}, u32[]{:S(2)}) copy-start(bf16[2048,1024]{1,0:T(8,128)(2,1)} %param.13) | copy-start | bytes 12582916
  167.6 75.1 %copy-start = (bf16[128,2048]{1,0:T(8,128)(2,1)S(1)}, bf16[128,2048]{1,0:T(8,128)(2,1)}, u32[]{:S(2)}) copy-start(bf16[128,2048]{1,0:T(8,128)(2,1)} %param.12) | copy-start | bytes 1572868
Sparse Core Ops, SparseCore 0:
  9.2 40.1 all-gather.3
  51.3 37.4 all-gather.5
  93.6 58.2 all-gather.7
  167.8 43.8 reduce-scatter.1
where the time goes:
time: 251 us; the launch traced here: 250 us
  waiting for transfers between devices  179 us (71%)
  blocking collectives  30.1 us (12%)
  local copies, waits for them, and re-layouts  18.4 us (7%)
  between operations  13.2 us (5%)
  matrix products  7.06 us (3%)
    all_gather x1, waiting for transfers between devices, per_device(): gathered = lax.all_gather(local_context, 'seq', axis=0, tiled=True)  58.4 us
    reduce_scatter x1, waiting for transfers between devices, per_device(): lax.psum_scatter(jnp.dot(rows, out_weight, preferred_element_type=jnp.flo...  44 us
    all_gather x1, waiting for transfers between devices, per_device(): piece_values = lax.all_gather(value_proj, 'seq', axis=0, tiled=True)  39.3 us
    all_gather x1, waiting for transfers between devices, per_device(): piece_keys = lax.all_gather(key_proj, 'seq', axis=0, tiled=True)  37 us
    all_to_all x1, blocking collectives, per_device(): lax.all_to_all(lax.all_to_all(partial_sums.astype(jnp.bfloat16), 'seq', s...  16.7 us
    all_to_all x1, blocking collectives, per_device(): lax.all_to_all(partial_sums.astype(jnp.bfloat16), 'seq', split_axis=0, co...  13.4 us
    all_gather x1, local copies, waits for them, and re-layouts, per_device(): gathered = lax.all_gather(local_context, 'seq', axis=0, tiled=True)  6.53 us
    unnamed x7, local copies, waits for them, and re-layouts  6.22 us
  transfers between devices with their start and end apart: 4, of which 4 were waited for; matrix products, arithmetic and copies ran while one was open for 1% of the time, Pallas kernels for 0%

commit v1 on v0

--- a/solution.py
+++ b/solution.py
@@ -5,6 +5,27 @@
 from jax.sharding import PartitionSpec as P
 
 HEAD_DIM = 128
+
+
+def gather_around(x, axis, dim):
+    peers, place, rows = (lax.axis_size(axis), lax.axis_index(axis), x.shape[dim])
+    right = [(i, (i + 1) % peers) for i in range(peers)]
+    downward = [(i, (i - 1) % peers) for i in range(peers)]
+    out = jnp.zeros((*x.shape[:dim], peers * rows, *x.shape[dim + 1 :]), x.dtype)
+    out = lax.dynamic_update_slice_in_dim(out, x, place * rows, axis=dim)
+    from_left = from_right = x
+    half = peers // 2
+    for step in range(1, half + 1):
+        from_left = lax.ppermute(from_left, axis, right)
+        out = lax.dynamic_update_slice_in_dim(
+            out, from_left, (place - step) % peers * rows, axis=dim
+        )
+        if step < peers - half:
+            from_right = lax.ppermute(from_right, axis, downward)
+            out = lax.dynamic_update_slice_in_dim(
+                out, from_right, (place + step) % peers * rows, axis=dim
+            )
+    return out
 
 
 def attend(state, query_rows, first_pos, key_block, value_block, block_start, score_scale):
@@ -67,7 +88,7 @@
         )
     )
     piece_keys = lax.all_gather(key_proj, "seq", axis=0, tiled=True)
-    piece_values = lax.all_gather(value_proj, "seq", axis=0, tiled=True)
+    piece_values = gather_around(value_proj, "seq", 0)
     piece_rows = piece_keys.shape[0]
 
     def one_block(block_index, states):

time: 251 us -> 234 us (0.932)
  waiting for transfers between devices: 179 us -> 139 us
  starting transfers between devices: 0.13 us -> 13.4 us
  local copies, waits for them, and re-layouts: 18.4 us -> 27.4 us
    all_gather x1 -> x0, waiting for transfers between devices: 39.3 us -> none  [per_device(): piece_values = lax.all_gather(value_proj, 'seq', axis=0, tiled=True)]
    ppermute x0 -> x7, waiting for transfers between devices: none -> 38.2 us  [the longest x4 23.6 us: gather_around(): from_left = lax.ppermute(from_left, axis, right)]
    all_gather x1, waiting for transfers between devices: 37 us -> 0.01 us  [per_device(): piece_keys = lax.all_gather(key_proj, 'seq', axis=0, tiled=True)]
    ppermute x0 -> x7, starting transfers between devices: none -> 13.4 us  [the longest x3 8.66 us: gather_around(): from_right = lax.ppermute(from_right, axis, downward)]
    dynamic_update_slice x0 -> x8, local copies, waits for them, and re-layouts: none -> 8.21 us  [the longest x3 3.73 us: gather_around(): lax.dynamic_update_slice_in_dim(out, from_right, (place + step) % peers *...]
    broadcast_in_dim x0 -> x1, local copies, waits for them, and re-layouts: none -> 2.52 us  [gather_around(): out = jnp.zeros((*x.shape[:dim], peers * rows, *x.shape[dim + 1:]), x.dtype)]
    unnamed x7 -> x9, local copies, waits for them, and re-layouts: 6.22 us -> 4.47 us
  transfers between devices with their start and end apart: 4 -> 10, of which waited for: 4 -> 8; matrix products, arithmetic and copies ran while one was open for 1% -> 5% of each run, Pallas kernels for 0% -> 0%
where the time goes in v1:
time: 234 us; the launch traced here: 233 us
  waiting for transfers between devices  139 us (59%)
  blocking collectives  30.1 us (13%)
  local copies, waits for them, and re-layouts  27.4 us (12%)
  starting transfers between devices  13.4 us (6%)
  between operations  13.2 us (6%)
  matrix products  7.08 us (3%)
    all_gather x1, waiting for transfers between devices, per_device(): gathered = lax.all_gather(local_context, 'seq', axis=0, tiled=True)  57 us
    reduce_scatter x1, waiting for transfers between devices, per_device(): lax.psum_scatter(jnp.dot(rows, out_weight, preferred_element_type=jnp.flo...  44 us
    ppermute x4, waiting for transfers between devices, gather_around(): from_left = lax.ppermute(from_left, axis, right)  23.6 us
    all_to_all x1, blocking collectives, per_device(): lax.all_to_all(lax.all_to_all(partial_sums.astype(jnp.bfloat16), 'seq', s...  16.7 us
    ppermute x3, waiting for transfers between devices, gather_around(): from_right = lax.ppermute(from_right, axis, downward)  14.6 us
    all_to_all x1, blocking collectives, per_device(): lax.all_to_all(partial_sums.astype(jnp.bfloat16), 'seq', split_axis=0, co...  13.4 us
    ppermute x3, starting transfers between devices, gather_around(): from_right = lax.ppermute(from_right, axis, downward)  8.66 us
    all_gather x1, local copies, waits for them, and re-layouts, per_device(): gathered = lax.all_gather(local_context, 'seq', axis=0, tiled=True)  6.56 us
  transfers between devices with their start and end apart: 10, of which 8 were waited for; matrix products, arithmetic and copies ran while one was open for 5% of the time, Pallas kernels for 0%

profile of v1, /device:TPU:0, one launch (start us, length us, event | category | flops | bytes accessed | tf_op | source)
XLA Modules:
  0.0 233.0 jit_solution(5083613361332113164)
XLA Ops:
  6.5 2.1 copy.36
  8.7 0.0 all-gather.5.cloned.1.call-start
  8.7 1.3 copy.38
  10.0 0.5 collective-permute-start
  10.5 2.9 %collective-permute-start.1 = (bf16[128,2048]{0,1:T(8,128)(2,1)S(1)}, bf16[128,2048]{0,1:T(8,128)(2,1)S(1)}, u32[]{:S(2)}, u32[]{:S(2)}) collective-permute-start(bf16[128,2048]{0,1:T(8,128)(2,1)S(1)} %copy.38), channel_id=1, source_target_pairs={{0,28},{4,0},{8,4},{12,8},{16,12},{20,16},{24,20},{28,24},{1,29},{... | collective-permute-start | bytes 1572872 | tf_op jit(solution)/shard_map/ppermute | solution.py:24
  13.5 9.8 %collective-permute-done = bf16[128,2048]{0,1:T(8,128)(2,1)S(1)} collective-permute-done((bf16[128,2048]{0,1:T(8,128)(2,1)S(1)}, bf16[128,2048]{0,1:T(8,128)(2,1)S(1)}, u32[]{:S(2)}, u32[]{:S(2)}) %collective-permute-start) | collective-permute-done | bytes 524320 | tf_op jit(solution)/shard_map/ppermute | solution.py:19
  23.2 4.2 %collective-permute-start.2 = (bf16[128,2048]{0,1:T(8,128)(2,1)S(1)}, bf16[128,2048]{0,1:T(8,128)(2,1)S(1)}, u32[]{:S(2)}, u32[]{:S(2)}) collective-permute-start(bf16[128,2048]{0,1:T(8,128)(2,1)S(1)} %collective-permute-done), channel_id=1, source_target_pairs={{0,4},{4,8},{8,12},{12,16},{16,20},{20,24},{24,28},{28,0},{1,5},{5... | collective-permute-start | bytes 1572872 | tf_op jit(solution)/shard_map/ppermute | solution.py:19
  27.4 3.0 %collective-permute-done.1 = bf16[128,2048]{0,1:T(8,128)(2,1)S(1)} collective-permute-done((bf16[128,2048]{0,1:T(8,128)(2,1)S(1)}, bf16[128,2048]{0,1:T(8,128)(2,1)S(1)}, u32[]{:S(2)}, u32[]{:S(2)}) %collective-permute-start.1) | collective-permute-done | bytes 524320 | tf_op jit(solution)/shard_map/ppermute | solution.py:24
  30.4 2.8 %collective-permute-start.3 = (bf16[128,2048]{0,1:T(8,128)(2,1)S(1)}, bf16[128,2048]{0,1:T(8,128)(2,1)}, u32[]{:S(2)}, u32[]{:S(2)}) collective-permute-start(bf16[128,2048]{0,1:T(8,128)(2,1)S(1)} %collective-permute-done.1), channel_id=1, source_target_pairs={{0,28},{4,0},{8,4},{12,8},{16,12},{20,16},{24,20},{28,24},{1,29},{... | collective-permute-start | bytes 1572872 | tf_op jit(solution)/shard_map/ppermute | solution.py:24
  33.2 2.5 %broadcast_in_dim.49 = bf16[1024,2048]{0,1:T(8,128)(2,1)} broadcast(bf16[]{:T(256)} %constant.127.clone.1), dimensions={} | broadcast | bytes 4194306 | tf_op jit(solution)/shard_map/broadcast_in_dim | solution.py:14
  35.8 0.9 constant_dynamic-update-slice_fusion.7
  36.7 0.3 copy.37
  36.9 0.3 copy.41
  37.3 0.9 collective-permute-done.2
  38.2 0.9 constant_dynamic-update-slice_fusion.6
  39.1 0.9 constant_dynamic-update-slice_fusion.5
  39.9 11.6 %collective-permute-done.3 = bf16[128,2048]{0,1:T(8,128)(2,1)} collective-permute-done((bf16[128,2048]{0,1:T(8,128)(2,1)S(1)}, bf16[128,2048]{0,1:T(8,128)(2,1)}, u32[]{:S(2)}, u32[]{:S(2)}) %collective-permute-start.3) | collective-permute-done | bytes 524320 | tf_op jit(solution)/shard_map/ppermute | solution.py:24
  51.5 2.9 %collective-permute-start.5 = (bf16[128,2048]{0,1:T(8,128)(2,1)}, bf16[128,2048]{0,1:T(8,128)(2,1)S(1)}, u32[]{:S(2)}, u32[]{:S(2)}) collective-permute-start(bf16[128,2048]{0,1:T(8,128)(2,1)} %collective-permute-done.3), channel_id=1, source_target_pairs={{0,28},{4,0},{8,4},{12,8},{16,12},{20,16},{24,20},{28,24},{1,29},{... | collective-permute-start | bytes 1572872 | tf_op jit(solution)/shard_map/ppermute | solution.py:24
  54.4 0.9 constant_dynamic-update-slice_fusion.4
  55.3 7.2 %collective-permute-done.4 = bf16[128,2048]{0,1:T(8,128)(2,1)S(1)} collective-permute-done((bf16[128,2048]{0,1:T(8,128)(2,1)S(1)}, bf16[128,2048]{0,1:T(8,128)(2,1)S(1)}, u32[]{:S(2)}, u32[]{:S(2)}) %collective-permute-start.4) | collective-permute-done | bytes 524320 | tf_op jit(solution)/shard_map/ppermute | solution.py:19
  62.5 1.9 constant_dynamic-update-slice_fusion.3
  64.5 0.9 constant_dynamic-update-slice_fusion.2
  65.4 0.9 constant_dynamic-update-slice_fusion.1
  66.3 5.7 %collective-permute-done.6 = bf16[128,2048]{0,1:T(8,128)(2,1)S(1)} collective-permute-done((bf16[128,2048]{0,1:T(8,128)(2,1)S(1)}, bf16[128,2048]{0,1:T(8,128)(2,1)S(1)}, u32[]{:S(2)}, u32[]{:S(2)}) %collective-permute-start.6) | collective-permute-done | bytes 524320 | tf_op jit(solution)/shard_map/ppermute | solution.py:19
  72.0 0.9 constant_dynamic-update-slice_fusion
  72.9 0.1 broadcast_in_dim.48
  73.1 3.3 %while.19 = (s32[]{:T(128)}, f32[16,128]{1,0:T(8,128)S(1)}, f32[16,128]{1,0:T(8,128)S(1)}, f32[16,128,128]{2,1,0:T(8,128)S(1)}, s32[]{:T(128)}, /*index=5*/s32[]...) while((s32[]{:T(128)}, f32[16,128]{1,0:T(8,128)S(1)}, ...), condition=%wide.region_5.6_spmd, body=%wide.region_0.5_spmd.sunk | while | flops 137122048 | bytes 9111853 | solution.py:109
  73.1 3.0 %conditional.2 = ((f32[16,128]{1,0:T(8,128)S(1)}, f32[16,128]{1,0:T(8,128)S(1)}, f32[16,128,128]{2,1,0:T(8,128)S(1)})) conditional(s32[]{:T(128)} %convert_element_type.63, (f32[16,128]{1,0:T(8,128)S(1)}, f32[16,128]{1,0:T(8,128)S(1)}, f32[16,128,128]{2,1,0:T(8,128)S(1)}) %tuple.61, (s32[]{:T(128)}, s32[]{:T(128)}, bf16[1024,2048]{0,1:T(8,128)(2,1)}, ...), branch_computations={%region_1.1_spmd, %region_2.4_spmd} | conditional | flops 137122048 | bytes 9111630 | solution.py:65
  73.1 1.3 constant_dynamic-slice_fusion
  74.4 0.1 broadcast_compare_fusion
  74.5 0.5 fusion.10
  75.0 0.2 fusion.3
  75.3 0.8 convolution_add_fusion
  76.4 0.3 copy.42
  76.7 0.9 divide_convert_fusion
  77.7 0.0 reduce-scatter.2.cloned.1.call-start
  77.8 57.0 %all-gather.5.cloned.1.call-done = bf16[1024,2048]{0,1:T(8,128)(2,1)} async-done(((bf16[128,2048]{0,1:T(8,128)(2,1)}), bf16[1024,2048]{0,1:T(8,128)(2,1)}) %all-gather.5.cloned.1.call-update) | async-done | bytes 4194320 | tf_op jit(solution)/shard_map/all_gather | solution.py:117
  134.7 6.6 %copy.43 = bf16[1024,2048]{1,0:T(8,128)(2,1)} copy(bf16[1024,2048]{0,1:T(8,128)(2,1)} %all-gather.5.cloned.1.call-done) | data formatting | bytes 8388608 | tf_op jit(solution)/shard_map/all_gather | solution.py:117
  141.3 2.7 %copy.44 = bf16[4,8,32,2048]{3,2,1,0:T(8,128)(2,1)S(1)} copy(bf16[4,8,32,2048]{3,2,0,1:T(8,128)(2,1)} %bitcast.29) | data formatting | bytes 8388608 | tf_op jit(solution)/shard_map/transpose | solution.py:121
  143.9 0.8 copy-done.2
  144.7 5.8 %convolution_convert_fusion = bf16[1024,1024]{1,0:T(8,128)(2,1)} fusion(bf16[1024,2048]{1,0:T(8,128)(2,1)S(1)} %bitcast.30, bf16[2048,1024]{1,0:T(8,128)(2,1)S(1)} %copy-done.2), kind=kOutput, calls=%fused_computation.18 | convolution fusion | flops 4296015872 | bytes 10485760 | tf_op jit(solution)/shard_map/dot_general | solution.py:123
  150.5 44.0 %reduce-scatter.2.cloned.1.call-done = bf16[256,1024]{1,0:T(8,128)(2,1)} async-done(((bf16[1024,1024]{1,0:T(8,128)(2,1)}), bf16[256,1024]{1,0:T(8,128)(2,1)}) %reduce-scatter.2.cloned.1.call-update) | async-done | bytes 524304 | tf_op jit(solution)/shard_map/reduce_scatter | solution.py:122
  194.5 13.4 %all_to_all.29 = bf16[8,32,1024]{2,1,0:T(8,128)(2,1)S(1)} all-to-all(bf16[8,32,1024]{2,1,0:T(8,128)(2,1)} %bitcast.34), channel_id=1, replica_groups=mesh['seq'=8,'chan'=4] {'seq'}, dimensions={0} | all-to-all | bytes 1048576 | tf_op jit(solution)/shard_map/all_to_all | solution.py:129
  207.9 0.3 copy.45
  208.2 0.4 all_to_all.25
  208.6 0.3 copy.46
  208.9 16.7 %all_to_all.30 = bf16[32,4,2048]{2,0,1:T(8,128)(2,1)S(1)} all-to-all(bf16[32,4,2048]{2,0,1:T(8,128)(2,1)S(1)} %copy.46), channel_id=1, replica_groups=mesh['seq'=8,'chan'=4] {'chan'}, dimensions={1} | all-to-all | bytes 1048576 | tf_op jit(solution)/shard_map/all_to_all | solution.py:128
  225.6 0.9 fusion.9
  (26 shorter events, 0.2 us)
Async XLA Ops:
  6.5 30.1 %copy-start.1 = (bf16[128,2048]{1,0:T(8,128)(2,1)S(1)}, bf16[128,2048]{1,0:T(8,128)(2,1)}, u32[]{:S(2)}) copy-start(bf16[128,2048]{1,0:T(8,128)(2,1)} %param.9) | copy-start | bytes 1572868
  6.5 66.4 %all-gather.3.cloned.1.call-start = ((), (), s32[]{:S(2)}) async-start(), calls=%async_computation.3 | async-start | bytes 4718592 | tf_op jit(solution)/shard_map/all_gather | solution.py:90
  8.7 126.1 %all-gather.5.cloned.1.call-start = ((), (), s32[]{:S(2)}) async-start(), calls=%async_computation.4 | async-start | bytes 4718592 | tf_op jit(solution)/shard_map/all_gather | solution.py:117
  10.0 13.2 %collective-permute-start = (bf16[128,2048]{0,1:T(8,128)(2,1)S(1)}, bf16[128,2048]{0,1:T(8,128)(2,1)S(1)}, u32[]{:S(2)}, u32[]{:S(2)}) collective-permute-start(bf16[128,2048]{0,1:T(8,128)(2,1)S(1)} %copy.38), channel_id=1, source_target_pairs={{0,4},{4,8},{8,12},{12,16},{16,20},{20,24},{24,28},{28,0},{1,5},{5... | collective-permute-start | bytes 1572872 | tf_op jit(solution)/shard_map/ppermute | solution.py:19
  10.5 19.9 %collective-permute-start.1 = (bf16[128,2048]{0,1:T(8,128)(2,1)S(1)}, bf16[128,2048]{0,1:T(8,128)(2,1)S(1)}, u32[]{:S(2)}, u32[]{:S(2)}) collective-permute-start(bf16[128,2048]{0,1:T(8,128)(2,1)S(1)} %copy.38), channel_id=1, source_target_pairs={{0,28},{4,0},{8,4},{12,8},{16,12},{20,16},{24,20},{28,24},{1,29},{... | collective-permute-start | bytes 1572872 | tf_op jit(solution)/shard_map/ppermute | solution.py:24
  23.2 14.9 %collective-permute-start.2 = (bf16[128,2048]{0,1:T(8,128)(2,1)S(1)}, bf16[128,2048]{0,1:T(8,128)(2,1)S(1)}, u32[]{:S(2)}, u32[]{:S(2)}) collective-permute-start(bf16[128,2048]{0,1:T(8,128)(2,1)S(1)} %collective-permute-done), channel_id=1, source_target_pairs={{0,4},{4,8},{8,12},{12,16},{16,20},{20,24},{24,28},{28,0},{1,5},{5... | collective-permute-start | bytes 1572872 | tf_op jit(solution)/shard_map/ppermute | solution.py:19
  30.4 21.1 %collective-permute-start.3 = (bf16[128,2048]{0,1:T(8,128)(2,1)S(1)}, bf16[128,2048]{0,1:T(8,128)(2,1)}, u32[]{:S(2)}, u32[]{:S(2)}) collective-permute-start(bf16[128,2048]{0,1:T(8,128)(2,1)S(1)} %collective-permute-done.1), channel_id=1, source_target_pairs={{0,28},{4,0},{8,4},{12,8},{16,12},{20,16},{24,20},{28,24},{1,29},{... | collective-permute-start | bytes 1572872 | tf_op jit(solution)/shard_map/ppermute | solution.py:24
  38.2 24.4 %collective-permute-start.4 = (bf16[128,2048]{0,1:T(8,128)(2,1)S(1)}, bf16[128,2048]{0,1:T(8,128)(2,1)S(1)}, u32[]{:S(2)}, u32[]{:S(2)}) collective-permute-start(bf16[128,2048]{0,1:T(8,128)(2,1)S(1)} %collective-permute-done.2), channel_id=1, source_target_pairs={{0,4},{4,8},{8,12},{12,16},{16,20},{20,24},{24,28},{28,0},{1,5},{5... | collective-permute-start | bytes 1572872 | tf_op jit(solution)/shard_map/ppermute | solution.py:19
  51.5 13.9 %collective-permute-start.5 = (bf16[128,2048]{0,1:T(8,128)(2,1)}, bf16[128,2048]{0,1:T(8,128)(2,1)S(1)}, u32[]{:S(2)}, u32[]{:S(2)}) collective-permute-start(bf16[128,2048]{0,1:T(8,128)(2,1)} %collective-permute-done.3), channel_id=1, source_target_pairs={{0,28},{4,0},{8,4},{12,8},{16,12},{20,16},{24,20},{28,24},{1,29},{... | collective-permute-start | bytes 1572872 | tf_op jit(solution)/shard_map/ppermute | solution.py:24
  62.5 9.5 %collective-permute-start.6 = (bf16[128,2048]{0,1:T(8,128)(2,1)S(1)}, bf16[128,2048]{0,1:T(8,128)(2,1)S(1)}, u32[]{:S(2)}, u32[]{:S(2)}) collective-permute-start(bf16[128,2048]{0,1:T(8,128)(2,1)S(1)} %collective-permute-done.4), channel_id=1, source_target_pairs={{0,4},{4,8},{8,12},{12,16},{16,20},{20,24},{24,28},{28,0},{1,5},{5... | collective-permute-start | bytes 1572872 | tf_op jit(solution)/shard_map/ppermute | solution.py:19
  77.7 116.8 %reduce-scatter.2.cloned.1.call-start = ((), (), s32[]{:S(2)}) async-start(), calls=%async_computation.5 | async-start | bytes 2621440 | tf_op jit(solution)/shard_map/reduce_scatter | solution.py:122
  141.3 3.4 %copy-start.2 = (bf16[2048,1024]{1,0:T(8,128)(2,1)S(1)}, bf16[2048,1024]{1,0:T(8,128)(2,1)}, u32[]{:S(2)}) copy-start(bf16[2048,1024]{1,0:T(8,128)(2,1)} %param.13) | copy-start | bytes 12582916
  150.5 75.1 %copy-start = (bf16[128,2048]{1,0:T(8,128)(2,1)S(1)}, bf16[128,2048]{1,0:T(8,128)(2,1)}, u32[]{:S(2)}) copy-start(bf16[128,2048]{1,0:T(8,128)(2,1)} %param.12) | copy-start | bytes 1572868
Sparse Core Ops, SparseCore 0:
  9.2 52.8 all-gather.2
  77.8 56.8 all-gather.4
  150.6 43.8 reduce-scatter.1
